TPU v7x, 128 devices: a whole 4x4x4 slice. The times are simulated.
128 devices in a mesh: pr: 8 (over z, core), pc: 16 (over y, x).
Axes of the slice: x: 4, y: 4, z: 4, core: 2. Of those that a mesh axis runs over, the one named last changes fastest.
Arguments:
- test_points: bfloat16 [131072, 512], P('pr'), may hold values from -15 to 15
- panel_points: bfloat16 [1024, 512], P('pc'), may hold values from -15 to 15
- factor_rows: float32 [1024, 32768], P('pc', 'pr'), may hold values from -0.03125 to 0.03125
- alpha_below: float32 [32768, 128], P(('pr', 'pc')), may hold values from -6 to 6
- targets: float32 [1024, 128], P('pc'), may hold values from -6 to 6
- inverse_block: float32 [1024, 1024], P('pc'), may hold values from -0.008 to 0.08, as said below
- predictions_in: float32 [131072, 128], P(('pr', 'pc')), may hold values from -6 to 6
Outputs:
- predictions: float32 [131072, 128], P(('pr', 'pc'))
Inputs may be any that keep to these rules, and one draw needn't show every extreme that they name: `inverse_block`: lower triangular with a positive diagonal.
All inputs are finite; a program needn't handle non-finite values.
Results may differ from a plain program's by a relative error of at most 0.0003.
Values may be sent and summed in bfloat16 or wider, within the bound.
No kernel may reach another device: no remote copies, remote signals or barrier semaphores. Data moves between devices by JAX's collectives and lax.ppermute only.
A program may use at most 128 MiB of HBM per device.

v0:
```python
import math
import jax
import jax.numpy as jnp
from jax import lax
from jax.sharding import PartitionSpec as P

LAYERS = 4
bias_var = 0.1
weight_var = 2.0


def arc_kernel(panel, test, test_norms):
    width = panel.shape[1]
    cross = jnp.dot(panel, test.T, preferred_element_type=jnp.float32) / width
    panel_var = jnp.einsum("pd,pd->p", panel, panel, preferred_element_type=jnp.float32) / width
    kern = bias_var + weight_var * cross
    panel_k = bias_var + weight_var * panel_var
    test_k = bias_var + weight_var * (test_norms / width)
    for level in range(LAYERS):
        spread = jnp.sqrt(panel_k[:, None] * test_k[None, :])
        cosine = kern / spread
        theta = jnp.arccos(cosine)
        kern = bias_var + weight_var / (2.0 * math.pi) * spread * (
            jnp.sqrt(1.0 - cosine * cosine) + (math.pi - theta) * cosine
        )
        panel_k = bias_var + 0.5 * weight_var * panel_k
        test_k = bias_var + 0.5 * weight_var * test_k
    return kern


def contract_rows(left, right):
    return lax.dot_general(
        left,
        right,
        (((0,), (0,)), ((), ())),
        precision=lax.Precision.HIGHEST,
        preferred_element_type=jnp.float32,
    )


def body(
    test_points, panel_points, factor_rows, alpha_below, targets, inverse_block, predictions_in
):
    partial_sum = jnp.dot(
        factor_rows,
        lax.all_gather(alpha_below, "pc", axis=0, tiled=True),
        precision=lax.Precision.HIGHEST,
        preferred_element_type=jnp.float32,
    )
    carried = lax.psum(partial_sum, "pr")
    residual = targets - carried
    alpha_panel = lax.psum_scatter(
        contract_rows(inverse_block, residual), "pc", scatter_dimension=0, tiled=True
    )
    test_norms = jnp.einsum(
        "nd,nd->n", test_points, test_points, preferred_element_type=jnp.float32
    )
    kern = arc_kernel(panel_points, test_points, test_norms)
    update = lax.psum_scatter(
        contract_rows(kern, alpha_panel), "pc", scatter_dimension=0, tiled=True
    )
    return predictions_in + update


def solution(mesh):
    placed = (
        P("pr", None),
        P("pc", None),
        P("pc", "pr"),
        P(("pr", "pc"), None),
        P("pc", None),
        P("pc", None),
        P(("pr", "pc"), None),
    )
    return jax.shard_map(
        body, mesh=mesh, in_specs=placed, out_specs=P(("pr", "pc"), None), check_vma=False
    )
```

profile of v0, /device:TPU:0, one launch (start us, length us, event | category | flops | bytes accessed | tf_op | source)
XLA Modules:
  0.0 328.8 jit_solution(5258146334610582226)
XLA Ops:
  6.5 0.0 copy-start
  6.5 0.0 all-gather.2.cloned.1.call-start
  6.5 0.7 all-gather.2.cloned.1.call-update
  7.3 0.0 reduce-scatter.7.cloned.1.call-start
  7.3 1.0 fusion.81
  8.3 0.0 copy-start.2
  8.3 0.0 copy-start.4
  8.3 7.2 %fusion = f32[16384]{0:T(1024)S(1)} fusion(bf16[16384,512]{1,0:T(8,128)(2,1)} %param.7), kind=kLoop, calls=%fused_computation.1 | loop fusion | flops 25149440 | bytes 16842752 | tf_op jit(solution)/shard_map/nd,nd->n/dot_general | solution.py:55
  15.5 0.0 copy-start.3
  15.6 41.2 %all-gather.2.cloned.1.call-done = f32[4096,128]{1,0:T(8,128)} async-done(((f32[256,128]{1,0:T(8,128)}), f32[4096,128]{1,0:T(8,128)}) %all-gather.2.cloned.1.call-update) | async-done | bytes 2097168 | tf_op jit(solution)/shard_map/all_gather | solution.py:46
  56.7 0.0 copy-done
  56.7 3.0 fusion.87
  59.7 24.3 %psum.7 = f32[64,128]{1,0:T(8,128)S(1)} all-reduce(f32[64,128]{1,0:T(8,128)S(1)} %fusion.87), channel_id=1, replica_groups=mesh['pr'=8,'pc'=16] {'pr'}, use_global_device_ids=true, to_apply=%region_0.0 | all-reduce | flops 8192 | bytes 65536 | tf_op jit(solution)/shard_map/psum | solution.py:50
  84.0 0.0 copy-done.2
  84.0 0.0 copy-done.4
  84.0 0.6 convolution_bitcast_fusion
  84.6 1.0 copy.16
  85.6 0.0 reduce-scatter.7.cloned.1.call-update
  85.7 0.0 reduce-scatter.5.cloned.1.call-start
  85.7 0.0 copy-done.3
  85.7 12.9 %fusion.2 = f32[64,16384]{1,0:T(8,128)} fusion(bf16[64,512]{1,0:T(8,128)(2,1)S(1)} %copy-done.3, bf16[16384,512]{1,0:T(8,128)(2,1)} %param.7, f32[16384]{0:T(1024)S(1)} %get-tuple-element.8, f32[64]{0:T(128)S(1)} %get-tuple-element.12), kind=kOutput, calls=%fused_computation.4 | convolution fusion | flops 1077936128 | bytes 21102848 | tf_op jit(solution)/shard_map/dot_general | solution.py:14
  98.6 57.3 %reduce-scatter.7.cloned.1.call-done = f32[64,128]{1,0:T(8,128)} async-done(((f32[1024,128]{1,0:T(8,128)}), f32[64,128]{1,0:T(8,128)}) %reduce-scatter.7.cloned.1.call-update) | async-done | bytes 32784
  156.0 78.8 %fusion.3 = f32[16384,128]{1,0:T(8,128)} fusion(f32[64,128]{1,0:T(8,128)} %reduce-scatter.7.cloned.1.call-done, f32[64,16384]{1,0:T(8,128)} %fusion.2, f32[16384]{0:T(1024)S(1)} %get-tuple-element.8, f32[64]{0:T(128)S(1)} %get-tuple-element.12, f32[16384]{0:T(1024)S(1)} %get-tuple-element.7, f32[64]{0:T(128)S(1)} %get-tuple-element.11, ...), kind=kOutput, calls=%fused_computation.5 | convolution fusion | flops 1664090112 | bytes 12878848 | tf_op jit(solution)/shard_map/dot_general | solution.py:32
  234.8 0.0 copy-start.1
  234.8 0.0 reduce-scatter.5.cloned.1.call-update
  234.8 85.3 %reduce-scatter.5.cloned.1.call-done = f32[1024,128]{1,0:T(8,128)} async-done(((f32[16384,128]{1,0:T(8,128)}), f32[1024,128]{1,0:T(8,128)}) %reduce-scatter.5.cloned.1.call-update) | async-done | bytes 524304 | tf_op jit(solution)/shard_map/reduce_scatter | solution.py:59
  320.0 0.0 copy-done.1
  320.0 1.9 add.111
  (2 shorter events, 0.0 us)
Async XLA Ops:
  6.5 50.2 %copy-start = (f32[64,4096]{1,0:T(8,128)S(1)}, f32[64,4096]{1,0:T(8,128)}, u32[]{:S(2)}) copy-start(f32[64,4096]{1,0:T(8,128)} %param.9) | copy-start | bytes 3145732
  6.5 50.2 %all-gather.2.cloned.1.call-start = ((), (), s32[]{:S(2)}) async-start(), calls=%async_computation.2 | async-start | bytes 2228224 | tf_op jit(solution)/shard_map/all_gather | solution.py:46
  7.3 148.7 %reduce-scatter.7.cloned.1.call-start = ((), (), s32[]{:S(2)}) async-start(), calls=%async_computation.4 | async-start | bytes 557056
  8.3 75.7 %copy-start.2 = (f32[64,1024]{1,0:T(8,128)S(1)}, f32[64,1024]{1,0:T(8,128)}, u32[]{:S(2)}) copy-start(f32[64,1024]{1,0:T(8,128)} %param.12) | copy-start | bytes 786436
  8.3 75.7 %copy-start.4 = (f32[64,128]{1,0:T(8,128)S(1)}, f32[64,128]{1,0:T(8,128)}, u32[]{:S(2)}) copy-start(f32[64,128]{1,0:T(8,128)} %param.11) | copy-start | bytes 98308
  15.5 70.2 %copy-start.3 = (bf16[64,512]{1,0:T(8,128)(2,1)S(1)}, bf16[64,512]{1,0:T(8,128)(2,1)}, u32[]{:S(2)}) copy-start(bf16[64,512]{1,0:T(8,128)(2,1)} %param.8) | copy-start | bytes 196612
  85.7 234.4 %reduce-scatter.5.cloned.1.call-start = ((), (), s32[]{:S(2)}) async-start(), calls=%async_computation.3 | async-start | bytes 8912896 | tf_op jit(solution)/shard_map/reduce_scatter | solution.py:59
  234.8 85.3 %copy-start.1 = (f32[1024,128]{1,0:T(8,128)S(1)}, f32[1024,128]{1,0:T(8,128)}, u32[]{:S(2)}) copy-start(f32[1024,128]{1,0:T(8,128)} %param.13) | copy-start | bytes 1572868
Sparse Core Ops, SparseCore 0:
  9.5 47.2 all-gather.1
  85.8 70.1 reduce-scatter.6
  234.9 85.0 reduce-scatter.4
where the time goes:
time: 334 us; the launch traced here: 329 us
  waiting for transfers between devices  184 us (55%)
  matrix products  95.3 us (29%)
  blocking collectives  24.3 us (7%)
  between operations  13.6 us (4%)
  other arithmetic  10.1 us (3%)
    reduce_scatter x1, waiting for transfers between devices, body(): lax.psum_scatter(contract_rows(kern, alpha_panel), 'pc', scatter_dimensio...  85.3 us
    dot_general x2, matrix products, contract_rows(): lax.dot_general(left, right, (((0,), (0,)), ((), ())), precision=lax.Prec...  79.4 us
    unnamed x4, waiting for transfers between devices  58.1 us
    all_gather x1, waiting for transfers between devices, body(): lax.all_gather(alpha_below, 'pc', axis=0, tiled=True)  41.2 us
    psum x1, blocking collectives, body(): carried = lax.psum(partial_sum, 'pr')  24.3 us
    dot_general x1, matrix products, arc_kernel(): cross = jnp.dot(panel, test.T, preferred_element_type=jnp.float32) / width  12.9 us
    dot_general x1, other arithmetic, body(): jnp.einsum('nd,nd->n', test_points, test_points, preferred_element_type=j...  7.24 us
  transfers between devices with their start and end apart: 3, of which 3 were waited for; matrix products, arithmetic and copies ran while one was open for 6% of the time, Pallas kernels for 0%

commit v1 on v0

--- a/solution.py
+++ b/solution.py
@@ -3,6 +3,7 @@
 import jax.numpy as jnp
 from jax import lax
 from jax.sharding import PartitionSpec as P
+from jax.lax import axis_size, ppermute
 
 LAYERS = 4
 bias_var = 0.1
@@ -41,13 +42,23 @@
 def body(
     test_points, panel_points, factor_rows, alpha_below, targets, inverse_block, predictions_in
 ):
+
+    def number_layers_all_on_mesh(sheet):
+        n_parts = axis_size("pr")
+        p_next = lambda before: [(m, m ^ before) for m in range(n_parts)]
+        odd = sheet
+        for t in range(n_parts.bit_length() - 1):
+            big = ppermute(odd, axis_name="pr", perm=p_next(1 << t))
+            odd = odd + big
+        return odd
+
     partial_sum = jnp.dot(
         factor_rows,
         lax.all_gather(alpha_below, "pc", axis=0, tiled=True),
         precision=lax.Precision.HIGHEST,
         preferred_element_type=jnp.float32,
     )
-    carried = lax.psum(partial_sum, "pr")
+    carried = number_layers_all_on_mesh(partial_sum)
     residual = targets - carried
     alpha_panel = lax.psum_scatter(
         contract_rows(inverse_block, residual), "pc", scatter_dimension=0, tiled=True

time: 334 us -> 324 us (0.970)
  blocking collectives: 24.3 us -> 0 us
  waiting for transfers between devices: 184 us -> 194 us
  starting transfers between devices: 0.08 us -> 4.87 us
    psum x1 -> x0, blocking collectives: 24.3 us -> none  [body(): carried = lax.psum(partial_sum, 'pr')]
    ppermute x0 -> x3, waiting for transfers between devices: none -> 5.67 us  [number_layers_all_on_mesh(): big = ppermute(odd, axis_name='pr', perm=p_next(1 << t))]
    ppermute x0 -> x3, starting transfers between devices: none -> 4.79 us  [number_layers_all_on_mesh(): big = ppermute(odd, axis_name='pr', perm=p_next(1 << t))]
  transfers between devices with their start and end apart: 3 -> 6, of which waited for: 3 -> 6; matrix products, arithmetic and copies ran while one was open for 6% -> 6% of each run, Pallas kernels for 0% -> 0%
where the time goes in v1:
time: 324 us; the launch traced here: 318 us
  waiting for transfers between devices  194 us (60%)
  matrix products  95.3 us (29%)
  between operations  13.6 us (4%)
  other arithmetic  9.27 us (3%)
  starting transfers between devices  4.87 us (2%)
    reduce_scatter x1, waiting for transfers between devices, body(): lax.psum_scatter(contract_rows(kern, alpha_panel), 'pc', scatter_dimensio...  85.3 us
    dot_general x2, matrix products, contract_rows(): lax.dot_general(left, right, (((0,), (0,)), ((), ())), precision=lax.Prec...  79.5 us
    unnamed x4, waiting for transfers between devices  60.7 us
    all_gather x1, waiting for transfers between devices, body(): lax.all_gather(alpha_below, 'pc', axis=0, tiled=True)  42.2 us
    dot_general x1, matrix products, arc_kernel(): cross = jnp.dot(panel, test.T, preferred_element_type=jnp.float32) / width  12.9 us
    dot_general x1, other arithmetic, body(): jnp.einsum('nd,nd->n', test_points, test_points, preferred_element_type=j...  7.23 us
  transfers between devices with their start and end apart: 6, of which 6 were waited for; matrix products, arithmetic and copies ran while one was open for 6% of the time, Pallas kernels for 0%

profile of v1, /device:TPU:0, one launch (start us, length us, event | category | flops | bytes accessed | tf_op | source)
XLA Modules:
  0.0 317.9 jit_solution(8048840663430292874)
XLA Ops:
  6.5 0.0 copy-start
  6.5 0.0 all-gather.2.cloned.1.call-start
  6.5 0.7 all-gather.2.cloned.1.call-update
  7.3 0.0 copy-start.3
  7.3 0.0 copy-start.2
  7.3 0.0 copy-start.4
  7.3 0.0 reduce-scatter.7.cloned.1.call-start
  7.3 7.2 %fusion = f32[16384]{0:T(1024)S(1)} fusion(bf16[16384,512]{1,0:T(8,128)(2,1)} %param.7), kind=kLoop, calls=%fused_computation.1 | loop fusion | flops 25149440 | bytes 16842752 | tf_op jit(solution)/shard_map/nd,nd->n/dot_general | solution.py:66
  14.6 42.2 %all-gather.2.cloned.1.call-done = f32[4096,128]{1,0:T(8,128)} async-done(((f32[256,128]{1,0:T(8,128)}), f32[4096,128]{1,0:T(8,128)}) %all-gather.2.cloned.1.call-update) | async-done | bytes 2097168 | tf_op jit(solution)/shard_map/all_gather | solution.py:57
  56.7 0.0 copy-done
  56.7 3.0 fusion.88
  59.7 0.1 collective-permute-start
  59.8 1.2 collective-permute-done
  61.0 1.6 collective-permute-start.1
  62.6 0.0 copy-done.3
  62.6 0.1 fusion.81
  62.7 2.2 collective-permute-done.1
  64.9 3.1 collective-permute-start.2
  68.1 2.3 collective-permute-done.2
  70.4 0.0 copy-done.2
  70.4 0.0 copy-done.4
  70.4 0.6 convolution_bitcast_fusion
  71.0 1.0 copy.16
  72.0 0.0 reduce-scatter.7.cloned.1.call-update
  72.0 0.0 reduce-scatter.5.cloned.1.call-start
  72.1 12.9 %fusion.2 = f32[64,16384]{1,0:T(8,128)} fusion(bf16[64,512]{1,0:T(8,128)(2,1)S(1)} %copy-done.3, bf16[16384,512]{1,0:T(8,128)(2,1)} %param.7, f32[16384]{0:T(1024)S(1)} %get-tuple-element.8, f32[64]{0:T(128)S(1)} %get-tuple-element.12), kind=kOutput, calls=%fused_computation.4 | convolution fusion | flops 1077936128 | bytes 21102848 | tf_op jit(solution)/shard_map/dot_general | solution.py:15
  85.0 59.9 %reduce-scatter.7.cloned.1.call-done = f32[64,128]{1,0:T(8,128)} async-done(((f32[1024,128]{1,0:T(8,128)}), f32[64,128]{1,0:T(8,128)}) %reduce-scatter.7.cloned.1.call-update) | async-done | bytes 32784
  144.9 78.8 %fusion.3 = f32[16384,128]{1,0:T(8,128)} fusion(f32[64,128]{1,0:T(8,128)} %reduce-scatter.7.cloned.1.call-done, f32[64,16384]{1,0:T(8,128)} %fusion.2, f32[16384]{0:T(1024)S(1)} %get-tuple-element.8, f32[64]{0:T(128)S(1)} %get-tuple-element.12, f32[16384]{0:T(1024)S(1)} %get-tuple-element.7, f32[64]{0:T(128)S(1)} %get-tuple-element.11, ...), kind=kOutput, calls=%fused_computation.5 | convolution fusion | flops 1664090112 | bytes 12878848 | tf_op jit(solution)/shard_map/dot_general | solution.py:33
  223.7 0.0 copy-start.1
  223.7 0.0 reduce-scatter.5.cloned.1.call-update
  223.8 85.3 %reduce-scatter.5.cloned.1.call-done = f32[1024,128]{1,0:T(8,128)} async-done(((f32[16384,128]{1,0:T(8,128)}), f32[1024,128]{1,0:T(8,128)}) %reduce-scatter.5.cloned.1.call-update) | async-done | bytes 524304 | tf_op jit(solution)/shard_map/reduce_scatter | solution.py:70
  309.1 0.0 copy-done.1
  309.1 1.9 add.121
  (4 shorter events, 0.0 us)
Async XLA Ops:
  6.5 50.2 %copy-start = (f32[64,4096]{1,0:T(8,128)S(1)}, f32[64,4096]{1,0:T(8,128)}, u32[]{:S(2)}) copy-start(f32[64,4096]{1,0:T(8,128)} %param.9) | copy-start | bytes 3145732
  6.5 50.2 %all-gather.2.cloned.1.call-start = ((), (), s32[]{:S(2)}) async-start(), calls=%async_computation.2 | async-start | bytes 2228224 | tf_op jit(solution)/shard_map/all_gather | solution.py:57
  7.3 55.3 %copy-start.3 = (bf16[64,512]{1,0:T(8,128)(2,1)S(1)}, bf16[64,512]{1,0:T(8,128)(2,1)}, u32[]{:S(2)}) copy-start(bf16[64,512]{1,0:T(8,128)(2,1)} %param.8) | copy-start | bytes 196612
  7.3 63.1 %copy-start.2 = (f32[64,1024]{1,0:T(8,128)S(1)}, f32[64,1024]{1,0:T(8,128)}, u32[]{:S(2)}) copy-start(f32[64,1024]{1,0:T(8,128)} %param.12) | copy-start | bytes 786436
  7.3 63.1 %copy-start.4 = (f32[64,128]{1,0:T(8,128)S(1)}, f32[64,128]{1,0:T(8,128)}, u32[]{:S(2)}) copy-start(f32[64,128]{1,0:T(8,128)} %param.11) | copy-start | bytes 98308
  7.3 137.6 %reduce-scatter.7.cloned.1.call-start = ((), (), s32[]{:S(2)}) async-start(), calls=%async_computation.4 | async-start | bytes 557056
  59.7 1.3 collective-permute-start
  61.0 3.9 %collective-permute-start.1 = (f32[64,128]{1,0:T(8,128)S(1)}, f32[64,128]{1,0:T(8,128)S(1)}, u32[]{:S(2)}, u32[]{:S(2)}) collective-permute-start(f32[64,128]{1,0:T(8,128)S(1)} %add.118), channel_id=1, source_target_pairs={{0,32},{16,48},{32,0},{48,16},{64,96},{80,112},{96,64},{112,80},{1... | collective-permute-start | bytes 98312 | tf_op jit(solution)/shard_map/ppermute | solution.py:51
  64.9 5.4 %collective-permute-start.2 = (f32[64,128]{1,0:T(8,128)S(1)}, f32[64,128]{1,0:T(8,128)S(1)}, u32[]{:S(2)}, u32[]{:S(2)}) collective-permute-start(f32[64,128]{1,0:T(8,128)S(1)} %add.119), channel_id=1, source_target_pairs={{0,64},{16,80},{32,96},{48,112},{64,0},{80,16},{96,32},{112,48},{1... | collective-permute-start | bytes 98312 | tf_op jit(solution)/shard_map/ppermute | solution.py:51
  72.0 237.1 %reduce-scatter.5.cloned.1.call-start = ((), (), s32[]{:S(2)}) async-start(), calls=%async_computation.3 | async-start | bytes 8912896 | tf_op jit(solution)/shard_map/reduce_scatter | solution.py:70
  223.7 85.4 %copy-start.1 = (f32[1024,128]{1,0:T(8,128)S(1)}, f32[1024,128]{1,0:T(8,128)}, u32[]{:S(2)}) copy-start(f32[1024,128]{1,0:T(8,128)} %param.13) | copy-start | bytes 1572868
Sparse Core Ops, SparseCore 0:
  9.5 47.2 all-gather.1
  72.1 72.7 reduce-scatter.6
  223.9 85.1 reduce-scatter.4
